TPU v7x, 256 devices: a whole 4x4x8 slice. The times are simulated.
256 devices in a mesh: dom: 16 (over z, core), grp: 16 (over y, x).
Axes of the slice: x: 4, y: 4, z: 8, core: 2. Of those that a mesh axis runs over, the one named last changes fastest.
Arguments:
- positions: float32 [65536, 3, 128], P(('dom', 'grp')), may hold values from -4 to 4
- velocities: float32 [65536, 3, 128], P(('dom', 'grp')), may hold values from -9 to 9
- masses: float32 [65536, 128], P(('dom', 'grp')), may hold values from 0.3 to 3
- destination: int32 [65536], P(('dom', 'grp')), may hold values from 0 to 15, as said below
- group_ids: int32 [65536, 128], P(('dom', 'grp')), may hold values from 0 to 1023, as said below
- boundary_set: int32 [256, 64], P(('dom', 'grp')), may hold values from 0 to 511, as said below
- send_list: int32 [256, 16, 16], P(('dom', 'grp')), may hold values from 0 to 63, as said below
- send_count: int32 [256, 16], P(('dom', 'grp')), may hold values from 0 to 16, as said below
- partners: int32 [131072, 4], P(('dom', 'grp')), may hold values from 0 to 767, as said below
Outputs:
- energy: float32 [65536, 128], P(('dom', 'grp'))
- group_kinetic: float32 [1024], replicated
Inputs may be any that keep to these rules, and one draw needn't show every extreme that they name: Each block of 256 leaves sends at most 32 leaves to one destination; in each dom index one destination receives exactly 32 leaves from every block. `group_ids`: the particles of block b carry the 16 group numbers 4 * b to 4 * b + 15, taken modulo 1024, each at least once and no others. `boundary_set`: each row holds 64 distinct slot numbers. `send_list`: each row of 16 holds distinct positions. `send_count`: A block sends nothing to its own grp index; in each dom index one grp index receives 16 from every other block. `partners`: each row holds 4 distinct entry numbers of combined.
All inputs are finite; a program needn't handle non-finite values.
Results may differ from a plain program's by a relative error of at most 0.0003.
Values sent between devices are 32-bit elements; how exact they have to be, the bound alone decides.
No kernel may reach another device: no remote copies, remote signals or barrier semaphores. Data moves between devices by JAX's collectives and lax.ppermute only.
A program may use at most 64 MiB of HBM per device.

v0:
```python
import jax
import jax.numpy as jnp
from jax import lax
from jax.sharding import PartitionSpec as P

GSPAN = 16
GROUP_DEV = 4
softening = 0.0025
exact = lax.Precision.HIGHEST


def select_rows(table, index):
    count = table.shape[0]
    flat = table.reshape(count, -1)
    picker = (index.reshape(-1)[:, None] == jnp.arange(count, dtype=jnp.int32)[None, :]).astype(
        jnp.float32
    )
    chosen = jnp.dot(picker, flat, precision=exact, preferred_element_type=jnp.float32)
    return chosen.reshape(index.shape + table.shape[1:])


def tile_potential(targets, sources):
    distance = softening
    for component in range(3):
        offset = targets[:, None, component, :, None] - sources[:, :, component, None, :]
        distance = distance + offset * offset
    weights = sources[:, :, 3, None, :] * lax.rsqrt(distance)
    return -jnp.sum(weights, axis=(1, 3))


def slot_potential(owned, combined, pair_index, coupling):
    slot_count = owned.shape[0]
    leaf_width = owned.shape[2]
    block_rows = max(32, slot_count // 16)

    def one_block(inputs):
        targets, indices = inputs
        sources = select_rows(combined, indices)
        return tile_potential(targets, sources)

    result = lax.map(
        one_block,
        (
            owned.reshape(slot_count // block_rows, block_rows, 4, leaf_width),
            pair_index.reshape(slot_count // block_rows, block_rows, pair_index.shape[1]),
        ),
    )
    return result.reshape(slot_count, leaf_width) * coupling


def shards(
    positions,
    velocities,
    masses,
    destination,
    group_ids,
    boundary_set,
    send_list,
    send_count,
    partners,
):
    owners = lax.axis_size("grp")
    leaves = positions.shape[0]
    leaf_width = positions.shape[2]
    capacity = 2 * leaves // owners
    slot_count = owners * capacity
    groups = GROUP_DEV * lax.axis_size("dom") * owners
    block_index = lax.axis_index("dom") * owners + lax.axis_index("grp")
    first_group = block_index * GROUP_DEV
    mass_flat = masses.reshape(-1)
    group_flat = group_ids.reshape(-1)
    speeds = jnp.transpose(velocities, (1, 0, 2)).reshape(3, -1)
    local_ids = (group_flat - first_group) % groups
    member = (jnp.arange(GSPAN, dtype=jnp.int32)[:, None] == local_ids[None, :]).astype(jnp.float32)
    place = (
        (first_group + jnp.arange(GSPAN, dtype=jnp.int32))[:, None] % groups
        == jnp.arange(groups, dtype=jnp.int32)[None, :]
    ).astype(jnp.float32)

    def group_sums(stats):
        local_sums = jnp.einsum(
            "kp,gp->kg", stats, member, precision=exact, preferred_element_type=jnp.float32
        )
        return jnp.dot(local_sums, place, precision=exact, preferred_element_type=jnp.float32)

    first_sums = group_sums(
        jnp.concatenate([mass_flat[None, :], mass_flat[None, :] * speeds], axis=0)
    )
    mass_total, momentum = lax.psum((first_sums[0], first_sums[1:]), ("dom", "grp"))
    bulk_velocity = momentum / mass_total[None, :]
    bulk_local = jnp.einsum(
        "kq,gq->kg", bulk_velocity, place, precision=exact, preferred_element_type=jnp.float32
    )
    per_particle = jnp.dot(bulk_local, member, precision=exact, preferred_element_type=jnp.float32)
    relative = speeds - per_particle
    kinetic = 0.5 * jnp.sum(relative * relative, axis=0)
    heat_sum = lax.psum(group_sums((mass_flat * kinetic)[None, :])[0], ("dom", "grp"))
    group_kinetic = heat_sum / mass_total
    onehot = (destination[:, None] == jnp.arange(owners, dtype=jnp.int32)[None, :]).astype(
        jnp.int32
    )
    leaf_rank = jnp.sum((jnp.cumsum(onehot, axis=0) - onehot) * onehot, axis=1)
    target = destination * capacity + leaf_rank
    payload = jnp.concatenate([positions, masses[:, None, :]], axis=1)
    placing = (jnp.arange(slot_count, dtype=jnp.int32)[:, None] == target[None, :]).astype(
        jnp.float32
    )
    outgoing = jnp.dot(
        placing, payload.reshape(leaves, -1), precision=exact, preferred_element_type=jnp.float32
    ).reshape(slot_count, 4, leaf_width)
    owned = lax.all_to_all(outgoing, "grp", split_axis=0, concat_axis=0, tiled=True)
    set_size = boundary_set.shape[1]
    per_peer = send_list.shape[2]
    boundary = select_rows(owned, boundary_set[0])
    every_set = lax.all_gather(boundary, "grp", axis=0, tiled=True)
    all_lists, all_counts = (
        lax.all_gather(send_list, "grp", axis=0, tiled=True),
        lax.all_gather(send_count, "grp", axis=0, tiled=True),
    )
    my_index = lax.axis_index("grp")
    my_lists = jnp.take(all_lists, my_index, axis=1)
    my_counts = jnp.take(all_counts, my_index, axis=1)
    positions_in = jnp.arange(owners, dtype=jnp.int32)[:, None] * set_size + my_lists
    remote = select_rows(every_set, positions_in)
    is_live = jnp.arange(per_peer, dtype=jnp.int32)[None, :] < my_counts[:, None]
    remote = jnp.where(is_live[:, :, None, None], remote, jnp.zeros_like(remote))
    remote = remote.reshape(owners * per_peer, 4, leaf_width)
    combined = jnp.concatenate([owned, remote], axis=0)
    coupling = 1.0 / (partners.shape[1] * leaf_width)
    potential = slot_potential(owned, combined, partners, coupling)
    returned = lax.all_to_all(potential, "grp", split_axis=0, concat_axis=0, tiled=True)
    own_potential = jnp.einsum(
        "sl,sp->lp", placing, returned, precision=exact, preferred_element_type=jnp.float32
    )
    energy = kinetic.reshape(leaves, leaf_width) + own_potential
    return (energy, group_kinetic)


def solution(mesh):
    in_specs = (
        P(("dom", "grp"), None, None),
        P(("dom", "grp"), None, None),
        P(("dom", "grp"), None),
        P(("dom", "grp")),
        P(("dom", "grp"), None),
        P(("dom", "grp"), None),
        P(("dom", "grp"), None, None),
        P(("dom", "grp"), None),
        P(("dom", "grp"), None),
    )
    out_specs = (P(("dom", "grp"), None), P())
    return jax.shard_map(shards, mesh=mesh, in_specs=in_specs, out_specs=out_specs, check_vma=False)
```

profile of v0, /device:TPU:1, one launch (start us, length us, event | category | flops | bytes accessed | tf_op | source)
XLA Modules:
  0.0 366.0 jit_solution(14305169449429546651)
XLA Ops:
  10.2 1.2 copy.63
  13.7 23.4 %all_to_all.14 = f32[512,4,128]{2,1,0:T(4,128)S(1)} all-to-all(f32[512,4,128]{2,1,0:T(4,128)S(1)} %copy.64), channel_id=1, replica_groups=mesh['dom'=16,'grp'=16] {'grp'}, dimensions={0} | all-to-all | bytes 2097152 | tf_op jit(solution)/shard_map/all_to_all | solution.py:111
  37.5 1.4 fusion.15
  39.4 1.6 fusion.9
  42.0 14.1 %all-gather = s32[16,1,16]{2,1,0:T(1,128)S(1)} all-gather(s32[1,1,16]{2,1,0:T(1,128)S(1)} %bitcast.158), channel_id=1, replica_groups=mesh['dom'=16,'grp'=16] {'grp'}, dimensions={0}, use_global_device_ids=true | all-gather | bytes 1088 | tf_op jit(solution)/shard_map/all_gather | solution.py:118
  56.6 17.3 %all_gather.10 = s32[16,16,16]{2,1,0:T(8,128)S(1)} all-gather(s32[1,16,16]{2,1,0:T(8,128)S(1)} %copy-done.7), channel_id=1, replica_groups=mesh['dom'=16,'grp'=16] {'grp'}, dimensions={0}, use_global_device_ids=true | all-gather | bytes 17408 | tf_op jit(solution)/shard_map/all_gather | solution.py:117
  73.9 89.0 %all-reduce = (f32[3,1024]{1,0:T(4,128)S(1)}, f32[1024]{0:T(1024)S(1)}) all-reduce(f32[3,1024]{1,0:T(4,128)S(1)} %slice.60, f32[1024]{0:T(1024)S(1)} %bitcast.154), channel_id=1, replica_groups=mesh['dom'=16,'grp'=16] {'dom','grp'}, use_global_device_ids=true, to_apply=%region_0.1 | all-reduce | flops 4096 | bytes 32768 | tf_op jit(solution)/shard_map/psum | solution.py:89
  165.0 1.9 copy.66
  166.9 1.3 fusion.10
  168.6 1.5 pad_maximum_fusion
  170.1 1.7 copy.70
  171.8 104.0 %while.12 = (s32[]{:T(128)}, f32[16,32,128]{2,1,0:T(8,128)S(1)}, s32[16,32,4]{1,0,2:T(8,128)}, f32[768,4,128]{0,2,1:T(8,128)S(1)}, f32[16,32,4,128]{3,2,1,0:T(4,128)S(1)}, /*index=5*/s32[]{:T(128)}) while((s32[]{:T(128)}, f32[16,32,128]{2,1,0:T(8,128)S(1)}, s32[16,32,4]{1,0,2:T(8,128)}, f32[768,4,128]{0,2,1:T(8,128)S(1)}, ...), condition=%wide.region_8.9_spmd, body=%wide.region_6.8_spmd.sunk | while | flops 627146752 | bytes 3606097 | solution.py:41
  174.0 4.4 %multiply_reduce_fusion.2 = f32[32,128]{1,0:T(8,128)S(1)} fusion(f32[32,4,128]{2,1,0:T(4,128)S(1)} %copy.88, f32[32,128]{1,0:T(8,128)S(1)} %get-tuple-element.135, f32[32,4,128]{2,1,0:T(4,128)S(1)} %copy.90, f32[32,128]{1,0:T(8,128)S(1)} %get-tuple-element.137, f32[32,4,128]{2,1,0:T(4,128)S(1)} %copy.91, f32[32,128]{1,0:T(8,128)S(1)} %get-tuple-element.139, ...), kind=kLoop, calls=%fused_computation.clone.1 | loop fusion | flops 23064576 | bytes 327680 | tf_op jit(solution)/shard_map/while/body/eval_jaxpr/reduce_sum | solution.py:28
  180.5 4.4 %multiply_reduce_fusion.2 = f32[32,128]{1,0:T(8,128)S(1)} fusion(f32[32,4,128]{2,1,0:T(4,128)S(1)} %copy.88, f32[32,128]{1,0:T(8,128)S(1)} %get-tuple-element.135, f32[32,4,128]{2,1,0:T(4,128)S(1)} %copy.90, f32[32,128]{1,0:T(8,128)S(1)} %get-tuple-element.137, f32[32,4,128]{2,1,0:T(4,128)S(1)} %copy.91, f32[32,128]{1,0:T(8,128)S(1)} %get-tuple-element.139, ...), kind=kLoop, calls=%fused_computation.clone.1 | loop fusion | flops 23064576 | bytes 327680 | tf_op jit(solution)/shard_map/while/body/eval_jaxpr/reduce_sum | solution.py:28
  187.0 4.4 %multiply_reduce_fusion.2 = f32[32,128]{1,0:T(8,128)S(1)} fusion(f32[32,4,128]{2,1,0:T(4,128)S(1)} %copy.88, f32[32,128]{1,0:T(8,128)S(1)} %get-tuple-element.135, f32[32,4,128]{2,1,0:T(4,128)S(1)} %copy.90, f32[32,128]{1,0:T(8,128)S(1)} %get-tuple-element.137, f32[32,4,128]{2,1,0:T(4,128)S(1)} %copy.91, f32[32,128]{1,0:T(8,128)S(1)} %get-tuple-element.139, ...), kind=kLoop, calls=%fused_computation.clone.1 | loop fusion | flops 23064576 | bytes 327680 | tf_op jit(solution)/shard_map/while/body/eval_jaxpr/reduce_sum | solution.py:28
  193.5 4.4 %multiply_reduce_fusion.2 = f32[32,128]{1,0:T(8,128)S(1)} fusion(f32[32,4,128]{2,1,0:T(4,128)S(1)} %copy.88, f32[32,128]{1,0:T(8,128)S(1)} %get-tuple-element.135, f32[32,4,128]{2,1,0:T(4,128)S(1)} %copy.90, f32[32,128]{1,0:T(8,128)S(1)} %get-tuple-element.137, f32[32,4,128]{2,1,0:T(4,128)S(1)} %copy.91, f32[32,128]{1,0:T(8,128)S(1)} %get-tuple-element.139, ...), kind=kLoop, calls=%fused_computation.clone.1 | loop fusion | flops 23064576 | bytes 327680 | tf_op jit(solution)/shard_map/while/body/eval_jaxpr/reduce_sum | solution.py:28
  200.0 4.4 %multiply_reduce_fusion.2 = f32[32,128]{1,0:T(8,128)S(1)} fusion(f32[32,4,128]{2,1,0:T(4,128)S(1)} %copy.88, f32[32,128]{1,0:T(8,128)S(1)} %get-tuple-element.135, f32[32,4,128]{2,1,0:T(4,128)S(1)} %copy.90, f32[32,128]{1,0:T(8,128)S(1)} %get-tuple-element.137, f32[32,4,128]{2,1,0:T(4,128)S(1)} %copy.91, f32[32,128]{1,0:T(8,128)S(1)} %get-tuple-element.139, ...), kind=kLoop, calls=%fused_computation.clone.1 | loop fusion | flops 23064576 | bytes 327680 | tf_op jit(solution)/shard_map/while/body/eval_jaxpr/reduce_sum | solution.py:28
  206.5 4.4 %multiply_reduce_fusion.2 = f32[32,128]{1,0:T(8,128)S(1)} fusion(f32[32,4,128]{2,1,0:T(4,128)S(1)} %copy.88, f32[32,128]{1,0:T(8,128)S(1)} %get-tuple-element.135, f32[32,4,128]{2,1,0:T(4,128)S(1)} %copy.90, f32[32,128]{1,0:T(8,128)S(1)} %get-tuple-element.137, f32[32,4,128]{2,1,0:T(4,128)S(1)} %copy.91, f32[32,128]{1,0:T(8,128)S(1)} %get-tuple-element.139, ...), kind=kLoop, calls=%fused_computation.clone.1 | loop fusion | flops 23064576 | bytes 327680 | tf_op jit(solution)/shard_map/while/body/eval_jaxpr/reduce_sum | solution.py:28
  213.0 4.4 %multiply_reduce_fusion.2 = f32[32,128]{1,0:T(8,128)S(1)} fusion(f32[32,4,128]{2,1,0:T(4,128)S(1)} %copy.88, f32[32,128]{1,0:T(8,128)S(1)} %get-tuple-element.135, f32[32,4,128]{2,1,0:T(4,128)S(1)} %copy.90, f32[32,128]{1,0:T(8,128)S(1)} %get-tuple-element.137, f32[32,4,128]{2,1,0:T(4,128)S(1)} %copy.91, f32[32,128]{1,0:T(8,128)S(1)} %get-tuple-element.139, ...), kind=kLoop, calls=%fused_computation.clone.1 | loop fusion | flops 23064576 | bytes 327680 | tf_op jit(solution)/shard_map/while/body/eval_jaxpr/reduce_sum | solution.py:28
  219.4 4.4 %multiply_reduce_fusion.2 = f32[32,128]{1,0:T(8,128)S(1)} fusion(f32[32,4,128]{2,1,0:T(4,128)S(1)} %copy.88, f32[32,128]{1,0:T(8,128)S(1)} %get-tuple-element.135, f32[32,4,128]{2,1,0:T(4,128)S(1)} %copy.90, f32[32,128]{1,0:T(8,128)S(1)} %get-tuple-element.137, f32[32,4,128]{2,1,0:T(4,128)S(1)} %copy.91, f32[32,128]{1,0:T(8,128)S(1)} %get-tuple-element.139, ...), kind=kLoop, calls=%fused_computation.clone.1 | loop fusion | flops 23064576 | bytes 327680 | tf_op jit(solution)/shard_map/while/body/eval_jaxpr/reduce_sum | solution.py:28
  225.9 4.4 %multiply_reduce_fusion.2 = f32[32,128]{1,0:T(8,128)S(1)} fusion(f32[32,4,128]{2,1,0:T(4,128)S(1)} %copy.88, f32[32,128]{1,0:T(8,128)S(1)} %get-tuple-element.135, f32[32,4,128]{2,1,0:T(4,128)S(1)} %copy.90, f32[32,128]{1,0:T(8,128)S(1)} %get-tuple-element.137, f32[32,4,128]{2,1,0:T(4,128)S(1)} %copy.91, f32[32,128]{1,0:T(8,128)S(1)} %get-tuple-element.139, ...), kind=kLoop, calls=%fused_computation.clone.1 | loop fusion | flops 23064576 | bytes 327680 | tf_op jit(solution)/shard_map/while/body/eval_jaxpr/reduce_sum | solution.py:28
  232.4 4.4 %multiply_reduce_fusion.2 = f32[32,128]{1,0:T(8,128)S(1)} fusion(f32[32,4,128]{2,1,0:T(4,128)S(1)} %copy.88, f32[32,128]{1,0:T(8,128)S(1)} %get-tuple-element.135, f32[32,4,128]{2,1,0:T(4,128)S(1)} %copy.90, f32[32,128]{1,0:T(8,128)S(1)} %get-tuple-element.137, f32[32,4,128]{2,1,0:T(4,128)S(1)} %copy.91, f32[32,128]{1,0:T(8,128)S(1)} %get-tuple-element.139, ...), kind=kLoop, calls=%fused_computation.clone.1 | loop fusion | flops 23064576 | bytes 327680 | tf_op jit(solution)/shard_map/while/body/eval_jaxpr/reduce_sum | solution.py:28
  238.9 4.4 %multiply_reduce_fusion.2 = f32[32,128]{1,0:T(8,128)S(1)} fusion(f32[32,4,128]{2,1,0:T(4,128)S(1)} %copy.88, f32[32,128]{1,0:T(8,128)S(1)} %get-tuple-element.135, f32[32,4,128]{2,1,0:T(4,128)S(1)} %copy.90, f32[32,128]{1,0:T(8,128)S(1)} %get-tuple-element.137, f32[32,4,128]{2,1,0:T(4,128)S(1)} %copy.91, f32[32,128]{1,0:T(8,128)S(1)} %get-tuple-element.139, ...), kind=kLoop, calls=%fused_computation.clone.1 | loop fusion | flops 23064576 | bytes 327680 | tf_op jit(solution)/shard_map/while/body/eval_jaxpr/reduce_sum | solution.py:28
  245.4 4.4 %multiply_reduce_fusion.2 = f32[32,128]{1,0:T(8,128)S(1)} fusion(f32[32,4,128]{2,1,0:T(4,128)S(1)} %copy.88, f32[32,128]{1,0:T(8,128)S(1)} %get-tuple-element.135, f32[32,4,128]{2,1,0:T(4,128)S(1)} %copy.90, f32[32,128]{1,0:T(8,128)S(1)} %get-tuple-element.137, f32[32,4,128]{2,1,0:T(4,128)S(1)} %copy.91, f32[32,128]{1,0:T(8,128)S(1)} %get-tuple-element.139, ...), kind=kLoop, calls=%fused_computation.clone.1 | loop fusion | flops 23064576 | bytes 327680 | tf_op jit(solution)/shard_map/while/body/eval_jaxpr/reduce_sum | solution.py:28
  251.9 4.4 %multiply_reduce_fusion.2 = f32[32,128]{1,0:T(8,128)S(1)} fusion(f32[32,4,128]{2,1,0:T(4,128)S(1)} %copy.88, f32[32,128]{1,0:T(8,128)S(1)} %get-tuple-element.135, f32[32,4,128]{2,1,0:T(4,128)S(1)} %copy.90, f32[32,128]{1,0:T(8,128)S(1)} %get-tuple-element.137, f32[32,4,128]{2,1,0:T(4,128)S(1)} %copy.91, f32[32,128]{1,0:T(8,128)S(1)} %get-tuple-element.139, ...), kind=kLoop, calls=%fused_computation.clone.1 | loop fusion | flops 23064576 | bytes 327680 | tf_op jit(solution)/shard_map/while/body/eval_jaxpr/reduce_sum | solution.py:28
  258.4 4.4 %multiply_reduce_fusion.2 = f32[32,128]{1,0:T(8,128)S(1)} fusion(f32[32,4,128]{2,1,0:T(4,128)S(1)} %copy.88, f32[32,128]{1,0:T(8,128)S(1)} %get-tuple-element.135, f32[32,4,128]{2,1,0:T(4,128)S(1)} %copy.90, f32[32,128]{1,0:T(8,128)S(1)} %get-tuple-element.137, f32[32,4,128]{2,1,0:T(4,128)S(1)} %copy.91, f32[32,128]{1,0:T(8,128)S(1)} %get-tuple-element.139, ...), kind=kLoop, calls=%fused_computation.clone.1 | loop fusion | flops 23064576 | bytes 327680 | tf_op jit(solution)/shard_map/while/body/eval_jaxpr/reduce_sum | solution.py:28
  264.9 4.4 %multiply_reduce_fusion.2 = f32[32,128]{1,0:T(8,128)S(1)} fusion(f32[32,4,128]{2,1,0:T(4,128)S(1)} %copy.88, f32[32,128]{1,0:T(8,128)S(1)} %get-tuple-element.135, f32[32,4,128]{2,1,0:T(4,128)S(1)} %copy.90, f32[32,128]{1,0:T(8,128)S(1)} %get-tuple-element.137, f32[32,4,128]{2,1,0:T(4,128)S(1)} %copy.91, f32[32,128]{1,0:T(8,128)S(1)} %get-tuple-element.139, ...), kind=kLoop, calls=%fused_computation.clone.1 | loop fusion | flops 23064576 | bytes 327680 | tf_op jit(solution)/shard_map/while/body/eval_jaxpr/reduce_sum | solution.py:28
  271.4 4.4 %multiply_reduce_fusion.2 = f32[32,128]{1,0:T(8,128)S(1)} fusion(f32[32,4,128]{2,1,0:T(4,128)S(1)} %copy.88, f32[32,128]{1,0:T(8,128)S(1)} %get-tuple-element.135, f32[32,4,128]{2,1,0:T(4,128)S(1)} %copy.90, f32[32,128]{1,0:T(8,128)S(1)} %get-tuple-element.137, f32[32,4,128]{2,1,0:T(4,128)S(1)} %copy.91, f32[32,128]{1,0:T(8,128)S(1)} %get-tuple-element.139, ...), kind=kLoop, calls=%fused_computation.clone.1 | loop fusion | flops 23064576 | bytes 327680 | tf_op jit(solution)/shard_map/while/body/eval_jaxpr/reduce_sum | solution.py:28
  276.5 3.5 all-to-all-start.1
  280.1 1.4 fusion.14
  281.7 75.6 %psum.23 = f32[1024]{0:T(1024)S(1)} all-reduce(f32[1024]{0:T(1024)S(1)} %bitcast.156), channel_id=1, replica_groups=mesh['dom'=16,'grp'=16] {'dom','grp'}, use_global_device_ids=true, to_apply=%region_9.10 | all-reduce | flops 1024 | bytes 8192 | tf_op jit(solution)/shard_map/psum | solution.py:97
  357.9 1.3 convolution_add_fusion
  (240 shorter events, 43.8 us)
Async XLA Ops:
  7.2 157.8 %all-gather.3.cloned.1.call-start = ((), (), s32[]{:S(2)}) async-start(), calls=%async_computation.2 | async-start | bytes 2228224 | tf_op jit(solution)/shard_map/all_gather | solution.py:115
  13.7 23.8 %copy-start.10 = (s32[1,64]{1,0:T(1,128)S(1)}, s32[1,64]{1,0:T(1,128)}, u32[]{:S(2)}) copy-start(s32[1,64]{1,0:T(1,128)} %param.16) | copy-start | bytes 772
  37.1 1.8 copy-start
  37.1 1.8 copy-start.1
  37.1 2.2 copy-start.3
  37.5 3.8 %copy-start.6 = (s32[512,4]{0,1:T(4,128)S(1)}, s32[512,4]{0,1:T(4,128)}, u32[]{:S(2)}) copy-start(s32[512,4]{0,1:T(4,128)} %param.19) | copy-start | bytes 24580
  37.5 4.5 %copy-start.11 = (s32[1,16]{1,0:T(1,128)S(1)}, s32[1,16]{1,0:T(1,128)}, u32[]{:S(2)}) copy-start(s32[1,16]{1,0:T(1,128)} %param.18) | copy-start | bytes 196
  37.5 19.0 %copy-start.7 = (s32[1,16,16]{2,1,0:T(8,128)S(1)}, s32[1,16,16]{2,1,0:T(8,128)}, u32[]{:S(2)}) copy-start(s32[1,16,16]{2,1,0:T(8,128)} %param.17) | copy-start | bytes 3076
  39.3 125.7 %copy-start.12 = (s32[16]{0:T(128)}, s32[16]{0:T(128)S(1)}, u32[]{:S(2)}) copy-start(s32[16]{0:T(128)S(1)} %and_select_fusion) | copy-start | bytes 196
  39.4 125.6 %copy-start.4 = (s32[32768]{0:T(1024)}, s32[32768]{0:T(1024)S(1)}, u32[]{:S(2)}) copy-start(s32[32768]{0:T(1024)S(1)} %add_select_fusion) | copy-start | bytes 393220
  162.8 1.4 copy-start.8
  171.8 108.3 %copy-start.2 = (f32[32768]{0:T(1024)S(1)}, f32[32768]{0:T(1024)}, u32[]{:S(2)}) copy-start(f32[32768]{0:T(1024)} %multiply_multiply_fusion) | copy-start | bytes 393220
  171.8 108.3 %copy-start.5 = (s32[32768]{0:T(1024)S(1)}, s32[32768]{0:T(1024)}, u32[]{:S(2)}) copy-start(s32[32768]{0:T(1024)} %copy-done.4) | copy-start | bytes 393220
  171.8 109.7 %copy-start.13 = (s32[16]{0:T(128)S(1)}, s32[16]{0:T(128)}, u32[]{:S(2)}) copy-start(s32[16]{0:T(128)} %copy-done.12) | copy-start | bytes 196
  171.8 185.5 %copy-start.9 = (f32[1024]{0:T(1024)S(1)}, f32[1024]{0:T(1024)}, u32[]{:S(2)}) copy-start(f32[1024]{0:T(1024)} %copy-done.8) | copy-start | bytes 12292
  276.5 81.4 %all-to-all-start.1 = ((f32[16,32,128]{2,1,0:T(8,128)}), f32[16,32,128]{2,1,0:T(8,128)S(1)}, u32[]{:S(2)}, u32[]{:S(2)}) async-start(f32[16,32,128]{2,1,0:T(8,128)} %broadcast_multiply_fusion), calls=%async_computation.1 | async-start | bytes 524288 | tf_op jit(solution)/shard_map/all_to_all | solution.py:131
Sparse Core Ops, SparseCore 0:
  39.0 48.9 all-gather.2
where the time goes:
time: 367 us; the launch traced here: 366 us
  blocking collectives  219 us (60%)
  other arithmetic  77.5 us (21%)
  matrix products  26 us (7%)
  local copies, waits for them, and re-layouts  23.5 us (6%)
  between operations  14.4 us (4%)
    psum x1, blocking collectives, shards(): lax.psum((first_sums[0], first_sums[1:]), ('dom', 'grp'))  89 us
    psum x1, blocking collectives, shards(): lax.psum(group_sums((mass_flat * kinetic)[None, :])[0], ('dom', 'grp'))  75.6 us
    reduce_sum x16, other arithmetic, tile_potential(): return -jnp.sum(weights, axis=(1, 3))  70.1 us
    all_to_all x1, blocking collectives, shards(): lax.all_to_all(outgoing, 'grp', split_axis=0, concat_axis=0, tiled=True)  23.4 us
    dot_general x18, matrix products, select_rows(): jnp.dot(picker, flat, precision=exact, preferred_element_type=jnp.float32)  19.3 us
    all_gather x1, blocking collectives, shards(): lax.all_gather(send_list, 'grp', axis=0, tiled=True)  17.3 us
    all_gather x1, blocking collectives, shards(): lax.all_gather(send_count, 'grp', axis=0, tiled=True)  14.1 us
    dynamic_slice x48, local copies, waits for them, and re-layouts, slot_potential(): lax.map(one_block, (owned.reshape(slot_count // block_rows, block_rows, 4...  12.1 us
  transfers between devices with their start and end apart: 2, of which 0 were waited for; matrix products, arithmetic and copies ran while one was open for 2% of the time, Pallas kernels for 0%

commit v1 on v0

--- a/solution.py
+++ b/solution.py
@@ -94,7 +94,9 @@
     per_particle = jnp.dot(bulk_local, member, precision=exact, preferred_element_type=jnp.float32)
     relative = speeds - per_particle
     kinetic = 0.5 * jnp.sum(relative * relative, axis=0)
-    heat_sum = lax.psum(group_sums((mass_flat * kinetic)[None, :])[0], ("dom", "grp"))
+    heat_sum = jnp.sum(
+        lax.all_gather(group_sums((mass_flat * kinetic)[None, :])[0], ("dom", "grp")), axis=0
+    )
     group_kinetic = heat_sum / mass_total
     onehot = (destination[:, None] == jnp.arange(owners, dtype=jnp.int32)[None, :]).astype(
         jnp.int32

time: 367 us -> 299 us (0.81)
  the two profiles are of different devices: /device:TPU:1 before, /device:TPU:2 now
where the time goes in v1:
time: 299 us; the launch traced here: 297 us
  blocking collectives  142 us (47%)
  other arithmetic  77 us (26%)
  matrix products  26.6 us (9%)
  local copies, waits for them, and re-layouts  24.8 us (8%)
  between operations  14.3 us (5%)
  starting transfers between devices  6.03 us (2%)
  waiting for transfers between devices  5.28 us (2%)
    psum x1, blocking collectives, shards(): lax.psum((first_sums[0], first_sums[1:]), ('dom', 'grp'))  77 us
    reduce_sum x16, other arithmetic, tile_potential(): return -jnp.sum(weights, axis=(1, 3))  70.1 us
    all_to_all x1, blocking collectives, shards(): lax.all_to_all(outgoing, 'grp', split_axis=0, concat_axis=0, tiled=True)  23.1 us
    all_gather x1, blocking collectives, shards(): lax.all_gather(send_list, 'grp', axis=0, tiled=True)  21.5 us
    all_gather x1, blocking collectives, shards(): lax.all_gather(send_count, 'grp', axis=0, tiled=True)  20.2 us
    dot_general x18, matrix products, select_rows(): jnp.dot(picker, flat, precision=exact, preferred_element_type=jnp.float32)  19.3 us
    dynamic_slice x48, local copies, waits for them, and re-layouts, slot_potential(): lax.map(one_block, (owned.reshape(slot_count // block_rows, block_rows, 4...  12 us
  transfers between devices with their start and end apart: 3, of which 1 were waited for; matrix products, arithmetic and copies ran while one was open for 40% of the time, Pallas kernels for 0%

profile of v1, /device:TPU:2, one launch (start us, length us, event | category | flops | bytes accessed | tf_op | source)
XLA Modules:
  0.0 297.4 jit_solution(3373814806902413359)
XLA Ops:
  13.7 23.1 %all_to_all.14 = f32[512,4,128]{2,1,0:T(4,128)S(1)} all-to-all(f32[512,4,128]{2,1,0:T(4,128)S(1)} %copy.64), channel_id=1, replica_groups=mesh['dom'=16,'grp'=16] {'grp'}, dimensions={0} | all-to-all | bytes 2097152 | tf_op jit(solution)/shard_map/all_to_all | solution.py:113
  37.1 1.4 fusion.15
  39.0 1.6 fusion.9
  40.9 77.0 %all-reduce = (f32[3,1024]{1,0:T(4,128)S(1)}, f32[1024]{0:T(1024)S(1)}) all-reduce(f32[3,1024]{1,0:T(4,128)S(1)} %slice.60, f32[1024]{0:T(1024)S(1)} %bitcast.154), channel_id=1, replica_groups=mesh['dom'=16,'grp'=16] {'dom','grp'}, use_global_device_ids=true, to_apply=%region_0.1 | all-reduce | flops 4096 | bytes 32768 | tf_op jit(solution)/shard_map/psum | solution.py:89
  119.3 1.4 fusion.14
  121.6 21.5 %all_gather.13 = s32[16,16,16]{2,1,0:T(8,128)S(1)} all-gather(s32[1,16,16]{2,1,0:T(8,128)S(1)} %copy-done.3), channel_id=1, replica_groups=mesh['dom'=16,'grp'=16] {'grp'}, dimensions={0}, use_global_device_ids=true | all-gather | bytes 17408 | tf_op jit(solution)/shard_map/all_gather | solution.py:119
  143.1 20.2 %all-gather.1 = s32[16,1,16]{2,1,0:T(1,128)S(1)} all-gather(s32[1,1,16]{2,1,0:T(1,128)S(1)} %bitcast.158), channel_id=1, replica_groups=mesh['dom'=16,'grp'=16] {'grp'}, dimensions={0}, use_global_device_ids=true | all-gather | bytes 1088 | tf_op jit(solution)/shard_map/all_gather | solution.py:120
  164.6 1.9 copy.66
  166.5 1.3 fusion.10
  168.2 1.5 pad_maximum_fusion
  169.7 1.7 copy.70
  171.4 103.9 %while.12 = (s32[]{:T(128)}, f32[16,32,128]{2,1,0:T(8,128)S(1)}, s32[16,32,4]{1,0,2:T(8,128)}, f32[768,4,128]{0,2,1:T(8,128)S(1)}, f32[16,32,4,128]{3,2,1,0:T(4,128)S(1)}, /*index=5*/s32[]{:T(128)}) while((s32[]{:T(128)}, f32[16,32,128]{2,1,0:T(8,128)S(1)}, s32[16,32,4]{1,0,2:T(8,128)}, f32[768,4,128]{0,2,1:T(8,128)S(1)}, ...), condition=%wide.region_8.9_spmd, body=%wide.region_6.8_spmd.sunk | while | flops 627146752 | bytes 3606097 | solution.py:41
  173.5 4.4 %multiply_reduce_fusion.2 = f32[32,128]{1,0:T(8,128)S(1)} fusion(f32[32,4,128]{2,1,0:T(4,128)S(1)} %copy.88, f32[32,128]{1,0:T(8,128)S(1)} %get-tuple-element.135, f32[32,4,128]{2,1,0:T(4,128)S(1)} %copy.90, f32[32,128]{1,0:T(8,128)S(1)} %get-tuple-element.137, f32[32,4,128]{2,1,0:T(4,128)S(1)} %copy.91, f32[32,128]{1,0:T(8,128)S(1)} %get-tuple-element.139, ...), kind=kLoop, calls=%fused_computation.clone.1 | loop fusion | flops 23064576 | bytes 327680 | tf_op jit(solution)/shard_map/while/body/eval_jaxpr/reduce_sum | solution.py:28
  180.0 4.4 %multiply_reduce_fusion.2 = f32[32,128]{1,0:T(8,128)S(1)} fusion(f32[32,4,128]{2,1,0:T(4,128)S(1)} %copy.88, f32[32,128]{1,0:T(8,128)S(1)} %get-tuple-element.135, f32[32,4,128]{2,1,0:T(4,128)S(1)} %copy.90, f32[32,128]{1,0:T(8,128)S(1)} %get-tuple-element.137, f32[32,4,128]{2,1,0:T(4,128)S(1)} %copy.91, f32[32,128]{1,0:T(8,128)S(1)} %get-tuple-element.139, ...), kind=kLoop, calls=%fused_computation.clone.1 | loop fusion | flops 23064576 | bytes 327680 | tf_op jit(solution)/shard_map/while/body/eval_jaxpr/reduce_sum | solution.py:28
  186.5 4.4 %multiply_reduce_fusion.2 = f32[32,128]{1,0:T(8,128)S(1)} fusion(f32[32,4,128]{2,1,0:T(4,128)S(1)} %copy.88, f32[32,128]{1,0:T(8,128)S(1)} %get-tuple-element.135, f32[32,4,128]{2,1,0:T(4,128)S(1)} %copy.90, f32[32,128]{1,0:T(8,128)S(1)} %get-tuple-element.137, f32[32,4,128]{2,1,0:T(4,128)S(1)} %copy.91, f32[32,128]{1,0:T(8,128)S(1)} %get-tuple-element.139, ...), kind=kLoop, calls=%fused_computation.clone.1 | loop fusion | flops 23064576 | bytes 327680 | tf_op jit(solution)/shard_map/while/body/eval_jaxpr/reduce_sum | solution.py:28
  193.0 4.4 %multiply_reduce_fusion.2 = f32[32,128]{1,0:T(8,128)S(1)} fusion(f32[32,4,128]{2,1,0:T(4,128)S(1)} %copy.88, f32[32,128]{1,0:T(8,128)S(1)} %get-tuple-element.135, f32[32,4,128]{2,1,0:T(4,128)S(1)} %copy.90, f32[32,128]{1,0:T(8,128)S(1)} %get-tuple-element.137, f32[32,4,128]{2,1,0:T(4,128)S(1)} %copy.91, f32[32,128]{1,0:T(8,128)S(1)} %get-tuple-element.139, ...), kind=kLoop, calls=%fused_computation.clone.1 | loop fusion | flops 23064576 | bytes 327680 | tf_op jit(solution)/shard_map/while/body/eval_jaxpr/reduce_sum | solution.py:28
  199.4 4.4 %multiply_reduce_fusion.2 = f32[32,128]{1,0:T(8,128)S(1)} fusion(f32[32,4,128]{2,1,0:T(4,128)S(1)} %copy.88, f32[32,128]{1,0:T(8,128)S(1)} %get-tuple-element.135, f32[32,4,128]{2,1,0:T(4,128)S(1)} %copy.90, f32[32,128]{1,0:T(8,128)S(1)} %get-tuple-element.137, f32[32,4,128]{2,1,0:T(4,128)S(1)} %copy.91, f32[32,128]{1,0:T(8,128)S(1)} %get-tuple-element.139, ...), kind=kLoop, calls=%fused_computation.clone.1 | loop fusion | flops 23064576 | bytes 327680 | tf_op jit(solution)/shard_map/while/body/eval_jaxpr/reduce_sum | solution.py:28
  205.9 4.4 %multiply_reduce_fusion.2 = f32[32,128]{1,0:T(8,128)S(1)} fusion(f32[32,4,128]{2,1,0:T(4,128)S(1)} %copy.88, f32[32,128]{1,0:T(8,128)S(1)} %get-tuple-element.135, f32[32,4,128]{2,1,0:T(4,128)S(1)} %copy.90, f32[32,128]{1,0:T(8,128)S(1)} %get-tuple-element.137, f32[32,4,128]{2,1,0:T(4,128)S(1)} %copy.91, f32[32,128]{1,0:T(8,128)S(1)} %get-tuple-element.139, ...), kind=kLoop, calls=%fused_computation.clone.1 | loop fusion | flops 23064576 | bytes 327680 | tf_op jit(solution)/shard_map/while/body/eval_jaxpr/reduce_sum | solution.py:28
  212.4 4.4 %multiply_reduce_fusion.2 = f32[32,128]{1,0:T(8,128)S(1)} fusion(f32[32,4,128]{2,1,0:T(4,128)S(1)} %copy.88, f32[32,128]{1,0:T(8,128)S(1)} %get-tuple-element.135, f32[32,4,128]{2,1,0:T(4,128)S(1)} %copy.90, f32[32,128]{1,0:T(8,128)S(1)} %get-tuple-element.137, f32[32,4,128]{2,1,0:T(4,128)S(1)} %copy.91, f32[32,128]{1,0:T(8,128)S(1)} %get-tuple-element.139, ...), kind=kLoop, calls=%fused_computation.clone.1 | loop fusion | flops 23064576 | bytes 327680 | tf_op jit(solution)/shard_map/while/body/eval_jaxpr/reduce_sum | solution.py:28
  218.9 4.4 %multiply_reduce_fusion.2 = f32[32,128]{1,0:T(8,128)S(1)} fusion(f32[32,4,128]{2,1,0:T(4,128)S(1)} %copy.88, f32[32,128]{1,0:T(8,128)S(1)} %get-tuple-element.135, f32[32,4,128]{2,1,0:T(4,128)S(1)} %copy.90, f32[32,128]{1,0:T(8,128)S(1)} %get-tuple-element.137, f32[32,4,128]{2,1,0:T(4,128)S(1)} %copy.91, f32[32,128]{1,0:T(8,128)S(1)} %get-tuple-element.139, ...), kind=kLoop, calls=%fused_computation.clone.1 | loop fusion | flops 23064576 | bytes 327680 | tf_op jit(solution)/shard_map/while/body/eval_jaxpr/reduce_sum | solution.py:28
  225.4 4.4 %multiply_reduce_fusion.2 = f32[32,128]{1,0:T(8,128)S(1)} fusion(f32[32,4,128]{2,1,0:T(4,128)S(1)} %copy.88, f32[32,128]{1,0:T(8,128)S(1)} %get-tuple-element.135, f32[32,4,128]{2,1,0:T(4,128)S(1)} %copy.90, f32[32,128]{1,0:T(8,128)S(1)} %get-tuple-element.137, f32[32,4,128]{2,1,0:T(4,128)S(1)} %copy.91, f32[32,128]{1,0:T(8,128)S(1)} %get-tuple-element.139, ...), kind=kLoop, calls=%fused_computation.clone.1 | loop fusion | flops 23064576 | bytes 327680 | tf_op jit(solution)/shard_map/while/body/eval_jaxpr/reduce_sum | solution.py:28
  231.9 4.4 %multiply_reduce_fusion.2 = f32[32,128]{1,0:T(8,128)S(1)} fusion(f32[32,4,128]{2,1,0:T(4,128)S(1)} %copy.88, f32[32,128]{1,0:T(8,128)S(1)} %get-tuple-element.135, f32[32,4,128]{2,1,0:T(4,128)S(1)} %copy.90, f32[32,128]{1,0:T(8,128)S(1)} %get-tuple-element.137, f32[32,4,128]{2,1,0:T(4,128)S(1)} %copy.91, f32[32,128]{1,0:T(8,128)S(1)} %get-tuple-element.139, ...), kind=kLoop, calls=%fused_computation.clone.1 | loop fusion | flops 23064576 | bytes 327680 | tf_op jit(solution)/shard_map/while/body/eval_jaxpr/reduce_sum | solution.py:28
  238.4 4.4 %multiply_reduce_fusion.2 = f32[32,128]{1,0:T(8,128)S(1)} fusion(f32[32,4,128]{2,1,0:T(4,128)S(1)} %copy.88, f32[32,128]{1,0:T(8,128)S(1)} %get-tuple-element.135, f32[32,4,128]{2,1,0:T(4,128)S(1)} %copy.90, f32[32,128]{1,0:T(8,128)S(1)} %get-tuple-element.137, f32[32,4,128]{2,1,0:T(4,128)S(1)} %copy.91, f32[32,128]{1,0:T(8,128)S(1)} %get-tuple-element.139, ...), kind=kLoop, calls=%fused_computation.clone.1 | loop fusion | flops 23064576 | bytes 327680 | tf_op jit(solution)/shard_map/while/body/eval_jaxpr/reduce_sum | solution.py:28
  244.9 4.4 %multiply_reduce_fusion.2 = f32[32,128]{1,0:T(8,128)S(1)} fusion(f32[32,4,128]{2,1,0:T(4,128)S(1)} %copy.88, f32[32,128]{1,0:T(8,128)S(1)} %get-tuple-element.135, f32[32,4,128]{2,1,0:T(4,128)S(1)} %copy.90, f32[32,128]{1,0:T(8,128)S(1)} %get-tuple-element.137, f32[32,4,128]{2,1,0:T(4,128)S(1)} %copy.91, f32[32,128]{1,0:T(8,128)S(1)} %get-tuple-element.139, ...), kind=kLoop, calls=%fused_computation.clone.1 | loop fusion | flops 23064576 | bytes 327680 | tf_op jit(solution)/shard_map/while/body/eval_jaxpr/reduce_sum | solution.py:28
  251.4 4.4 %multiply_reduce_fusion.2 = f32[32,128]{1,0:T(8,128)S(1)} fusion(f32[32,4,128]{2,1,0:T(4,128)S(1)} %copy.88, f32[32,128]{1,0:T(8,128)S(1)} %get-tuple-element.135, f32[32,4,128]{2,1,0:T(4,128)S(1)} %copy.90, f32[32,128]{1,0:T(8,128)S(1)} %get-tuple-element.137, f32[32,4,128]{2,1,0:T(4,128)S(1)} %copy.91, f32[32,128]{1,0:T(8,128)S(1)} %get-tuple-element.139, ...), kind=kLoop, calls=%fused_computation.clone.1 | loop fusion | flops 23064576 | bytes 327680 | tf_op jit(solution)/shard_map/while/body/eval_jaxpr/reduce_sum | solution.py:28
  257.9 4.4 %multiply_reduce_fusion.2 = f32[32,128]{1,0:T(8,128)S(1)} fusion(f32[32,4,128]{2,1,0:T(4,128)S(1)} %copy.88, f32[32,128]{1,0:T(8,128)S(1)} %get-tuple-element.135, f32[32,4,128]{2,1,0:T(4,128)S(1)} %copy.90, f32[32,128]{1,0:T(8,128)S(1)} %get-tuple-element.137, f32[32,4,128]{2,1,0:T(4,128)S(1)} %copy.91, f32[32,128]{1,0:T(8,128)S(1)} %get-tuple-element.139, ...), kind=kLoop, calls=%fused_computation.clone.1 | loop fusion | flops 23064576 | bytes 327680 | tf_op jit(solution)/shard_map/while/body/eval_jaxpr/reduce_sum | solution.py:28
  264.4 4.4 %multiply_reduce_fusion.2 = f32[32,128]{1,0:T(8,128)S(1)} fusion(f32[32,4,128]{2,1,0:T(4,128)S(1)} %copy.88, f32[32,128]{1,0:T(8,128)S(1)} %get-tuple-element.135, f32[32,4,128]{2,1,0:T(4,128)S(1)} %copy.90, f32[32,128]{1,0:T(8,128)S(1)} %get-tuple-element.137, f32[32,4,128]{2,1,0:T(4,128)S(1)} %copy.91, f32[32,128]{1,0:T(8,128)S(1)} %get-tuple-element.139, ...), kind=kLoop, calls=%fused_computation.clone.1 | loop fusion | flops 23064576 | bytes 327680 | tf_op jit(solution)/shard_map/while/body/eval_jaxpr/reduce_sum | solution.py:28
  270.9 4.4 %multiply_reduce_fusion.2 = f32[32,128]{1,0:T(8,128)S(1)} fusion(f32[32,4,128]{2,1,0:T(4,128)S(1)} %copy.88, f32[32,128]{1,0:T(8,128)S(1)} %get-tuple-element.135, f32[32,4,128]{2,1,0:T(4,128)S(1)} %copy.90, f32[32,128]{1,0:T(8,128)S(1)} %get-tuple-element.137, f32[32,4,128]{2,1,0:T(4,128)S(1)} %copy.91, f32[32,128]{1,0:T(8,128)S(1)} %get-tuple-element.139, ...), kind=kLoop, calls=%fused_computation.clone.1 | loop fusion | flops 23064576 | bytes 327680 | tf_op jit(solution)/shard_map/while/body/eval_jaxpr/reduce_sum | solution.py:28
  276.0 6.0 %all-to-all-start.1 = ((f32[16,32,128]{2,1,0:T(8,128)}), f32[16,32,128]{2,1,0:T(8,128)S(1)}, u32[]{:S(2)}, u32[]{:S(2)}) async-start(f32[16,32,128]{2,1,0:T(8,128)} %broadcast_multiply_fusion), calls=%async_computation.1 | async-start | bytes 524288 | tf_op jit(solution)/shard_map/all_to_all | solution.py:133
  282.0 1.4 reshape.284
  284.1 5.2 %all-to-all-done.1 = f32[16,32,128]{2,1,0:T(8,128)S(1)} async-done(((f32[16,32,128]{2,1,0:T(8,128)}), f32[16,32,128]{2,1,0:T(8,128)S(1)}, u32[]{:S(2)}, u32[]{:S(2)}) %all-to-all-start.1) | async-done | bytes 262176 | tf_op jit(solution)/shard_map/all_to_all | solution.py:133
  289.3 1.3 convolution_add_fusion
  (234 shorter events, 45.0 us)
Async XLA Ops:
  7.2 157.5 %all-gather.5.cloned.1.call-start = ((), (), s32[]{:S(2)}) async-start(), calls=%async_computation.2 | async-start | bytes 2228224 | tf_op jit(solution)/shard_map/all_gather | solution.py:117
  13.7 23.5 %copy-start.7 = (s32[1,64]{1,0:T(1,128)S(1)}, s32[1,64]{1,0:T(1,128)}, u32[]{:S(2)}) copy-start(s32[1,64]{1,0:T(1,128)} %param.16) | copy-start | bytes 772
  36.7 1.8 copy-start
  36.7 1.8 copy-start.1
  36.7 2.2 copy-start.2
  38.5 243.5 %all-gather.7.cloned.1.call-start = ((), (), s32[]{:S(2)}) async-start(), calls=%async_computation.3 | async-start | bytes 1052672 | tf_op jit(solution)/shard_map/all_gather | solution.py:98
  39.0 82.6 %copy-start.3 = (s32[1,16,16]{2,1,0:T(8,128)S(1)}, s32[1,16,16]{2,1,0:T(8,128)}, u32[]{:S(2)}) copy-start(s32[1,16,16]{2,1,0:T(8,128)} %param.17) | copy-start | bytes 3076
  39.0 104.1 %copy-start.8 = (s32[1,16]{1,0:T(1,128)S(1)}, s32[1,16]{1,0:T(1,128)}, u32[]{:S(2)}) copy-start(s32[1,16]{1,0:T(1,128)} %param.18) | copy-start | bytes 196
  39.0 124.8 %copy-start.4 = (s32[512,4]{0,1:T(4,128)S(1)}, s32[512,4]{0,1:T(4,128)}, u32[]{:S(2)}) copy-start(s32[512,4]{0,1:T(4,128)} %param.19) | copy-start | bytes 24580
  118.0 46.6 %copy-start.5 = (f32[1024]{0:T(1024)}, f32[1024]{0:T(1024)S(1)}, u32[]{:S(2)}) copy-start(f32[1024]{0:T(1024)S(1)} %get-tuple-element.88) | copy-start | bytes 12292
  275.3 8.2 %copy-start.6 = (f32[1024]{0:T(1024)S(1)}, f32[1024]{0:T(1024)}, u32[]{:S(2)}) copy-start(f32[1024]{0:T(1024)} %copy-done.5) | copy-start | bytes 12292
  276.0 13.3 %all-to-all-start.1 = ((f32[16,32,128]{2,1,0:T(8,128)}), f32[16,32,128]{2,1,0:T(8,128)S(1)}, u32[]{:S(2)}, u32[]{:S(2)}) async-start(f32[16,32,128]{2,1,0:T(8,128)} %broadcast_multiply_fusion), calls=%async_computation.1 | async-start | bytes 524288 | tf_op jit(solution)/shard_map/all_to_all | solution.py:133
Sparse Core Ops, SparseCore 0:
  38.6 49.7 all-gather.4
  121.7 99.1 all-gather.6
